TPU v7x, 512 devices: a whole 4x4x16 slice. The times are simulated.
512 devices in a mesh: pipe: 16 (over z), seq: 8 (over y, core), dp: 4 (over x).
Axes of the slice: x: 4, y: 4, z: 16, core: 2. Of those that a mesh axis runs over, the one named last changes fastest.
Arguments:
- acts: bfloat16 [16, 4, 1024, 8192], P('pipe', 'dp', 'seq'), may hold values from -6 to 6
- top_grad: bfloat16 [4, 1024, 8192], P('dp', 'seq'), may hold values from -6 to 6
- a_rows: bfloat16 [16, 32, 8192], P('pipe', None, ('seq', 'dp')), may hold values from -1 to 1
- b_rows: bfloat16 [16, 32, 8192], P('pipe', None, ('seq', 'dp')), may hold values from -0.375 to 0.375
- gain: bfloat16 [16, 8192], P('pipe', ('seq', 'dp')), may hold values from 0.5 to 1.5
Outputs:
- grad_a: float32 [16, 32, 8192], P('pipe', None, ('seq', 'dp'))
- grad_b: float32 [16, 32, 8192], P('pipe', None, ('seq', 'dp'))
- grad_gain: float32 [16, 8192], P('pipe', ('seq', 'dp'))
- clip_factors: float32 [4], P('dp')
All inputs are finite; a program needn't handle non-finite values.
Results may differ from a plain program's by a relative error of at most 0.019.
Values may be sent and summed in bfloat16 or wider, within the bound.
No kernel may reach another device: no remote copies, remote signals or barrier semaphores. Data moves between devices by JAX's collectives and lax.ppermute only.
A program may use at most 64 MiB of HBM per device.

v0:
```python
import math
import jax
import jax.numpy as jnp
from jax import lax
from jax.sharding import PartitionSpec as P

rows_per_block = 16


def from_behind(value, axis, steps):
    count = lax.axis_size(axis)
    initial, last = (max(0, -steps), min(count, count - steps))
    return lax.ppermute(value, axis, [(source, source + steps) for source in range(initial, last)])


def on_device(acts, top_grad, a_rows, b_rows, gain):
    sections = lax.axis_size("pipe")
    section = lax.axis_index("pipe")
    hidden = acts[0, 0]
    top = top_grad[0]
    rank = a_rows.shape[1]
    params = jnp.concatenate([a_rows[0], b_rows[0], gain], axis=0)
    whole = lax.all_gather(params, ("seq", "dp"), axis=1, tiled=True)
    a_full = whole[:rank]
    b_full = whole[rank : 2 * rank]
    gain_float = whole[2 * rank].astype(jnp.float32)
    rows, width = hidden.shape
    block_total = rows // rows_per_block
    hidden_float = hidden.astype(jnp.float32)
    inverse_root_mean = jnp.sqrt(
        jnp.mean(hidden_float * hidden_float, axis=-1, keepdims=True) + 1e-05
    )
    input_normalized = hidden_float / inverse_root_mean
    normalized_rows = (input_normalized * gain_float).astype(jnp.bfloat16)
    low = jnp.dot(normalized_rows, a_full.T, preferred_element_type=jnp.float32).astype(
        jnp.bfloat16
    )
    contract_last = (((1,), (1,)), ((), ()))
    contract_first = (((0,), (0,)), ((), ()))

    def back_block(upstream_gradient, block_offset):
        hidden_part = lax.dynamic_slice_in_dim(hidden, block_offset, rows_per_block, 0)
        r_part = lax.dynamic_slice_in_dim(inverse_root_mean, block_offset, rows_per_block, 0)
        input_portion = hidden_part.astype(jnp.float32) / r_part
        d_low = lax.dot_general(
            upstream_gradient, b_full, contract_last, preferred_element_type=jnp.float32
        ).astype(jnp.bfloat16)
        normalized_gradient = jnp.dot(d_low, a_full, preferred_element_type=jnp.float32)
        input_gradient = normalized_gradient * gain_float
        hidden_gradient = (
            upstream_gradient.astype(jnp.float32)
            + (
                input_gradient
                - input_portion * jnp.mean(input_gradient * input_portion, axis=-1, keepdims=True)
            )
            / r_part
        )
        return hidden_gradient.astype(jnp.bfloat16)

    def turn(turn_index, carry):
        incoming, store = carry
        block_index = turn_index - (sections - 1 - section)
        inside = jnp.logical_and(block_index >= 0, block_index < block_total)
        block_offset = jnp.clip(block_index, 0, block_total - 1) * rows_per_block
        top_block = lax.dynamic_slice_in_dim(top, block_offset, rows_per_block, 0)
        source = jnp.where(section == sections - 1, top_block, incoming)
        slot = jnp.where(inside, block_index, block_total)
        store = lax.dynamic_update_slice_in_dim(store, source[None], slot, 0)
        result = back_block(source, block_offset)
        incoming = from_behind(result, "pipe", -1)
        return (incoming, store)

    begin = (
        jnp.zeros((rows_per_block, width), jnp.bfloat16),
        jnp.zeros((block_total + 1, rows_per_block, width), jnp.bfloat16),
    )
    store = lax.fori_loop(0, sections + block_total - 1, turn, begin)[1]
    mine = store[:block_total].reshape(rows, width)
    d_low = lax.dot_general(mine, b_full, contract_last, preferred_element_type=jnp.float32).astype(
        jnp.bfloat16
    )
    normalized_gradient = jnp.dot(d_low, a_full, preferred_element_type=jnp.float32)
    grad_a = lax.dot_general(
        d_low, normalized_rows, contract_first, preferred_element_type=jnp.float32
    )
    grad_b = lax.dot_general(low, mine, contract_first, preferred_element_type=jnp.float32)
    gain_gradient = jnp.sum(normalized_gradient * input_normalized, axis=0)[None, :]
    grads = jnp.concatenate([grad_a, grad_b, gain_gradient], axis=0)
    part = lax.psum_scatter(grads, "seq", scatter_dimension=1, tiled=True)
    examples = lax.axis_size("dp")
    example = lax.axis_index("dp")
    square = jnp.sum(part * part)
    squares = jnp.where(jnp.arange(examples) == example, square, 0.0).astype(jnp.float32)
    totals = lax.psum(squares, ("pipe", "seq", "dp"))
    bound = math.sqrt(sections * (2 * rank + 1) * width)
    factors = bound / (jnp.sqrt(totals) + 0.01 * bound)
    gathered = lax.all_gather(part, "dp", axis=0, tiled=False)
    share = part.shape[1] // examples
    pieces = lax.dynamic_slice_in_dim(gathered, example * share, share, 2)
    combined = jnp.sum(factors[:, None, None] * pieces, axis=0)
    out_a = combined[:rank]
    out_b = combined[rank : 2 * rank]
    out_g = combined[2 * rank :]
    factor = lax.dynamic_slice_in_dim(factors, example, 1, 0)
    return (out_a[None], out_b[None], out_g, factor)


def solution(mesh):
    in_specs = (
        P("pipe", "dp", "seq", None),
        P("dp", "seq", None),
        P("pipe", None, ("seq", "dp")),
        P("pipe", None, ("seq", "dp")),
        P("pipe", ("seq", "dp")),
    )
    out_specs = (
        P("pipe", None, ("seq", "dp")),
        P("pipe", None, ("seq", "dp")),
        P("pipe", ("seq", "dp")),
        P("dp"),
    )
    return jax.shard_map(
        on_device, mesh=mesh, in_specs=in_specs, out_specs=out_specs, check_vma=False
    )
```

profile of v0, /device:TPU:1, one launch (start us, length us, event | category | flops | bytes accessed | tf_op | source)
XLA Modules:
  0.0 594.1 jit_solution(15978239011922078406)
XLA Ops:
  8.7 2.1 fusion.1
  10.8 64.3 %all-gather.5.cloned.1.call-done = bf16[65,8192]{1,0:T(8,128)(2,1)} async-done(((bf16[65,256]{1,0:T(8,128)(2,1)}), bf16[65,8192]{1,0:T(8,128)(2,1)}) %all-gather.5.cloned.1.call-update) | async-done | bytes 1064976 | tf_op jit(solution)/shard_map/all_gather | solution.py:23
  76.0 2.2 fusion.11
  78.5 318.4 %while.17 = (s32[]{:T(128)}, bf16[16,8192]{1,0:T(8,128)(2,1)S(1)}, bf16[9,16,8192]{2,1,0:T(8,128)(2,1)S(1)}, pred[]{:T(512)}, s32[]{:T(128)}, /*index=5*/bf16[12...) while((s32[]{:T(128)}, bf16[16,8192]{1,0:T(8,128)(2,1)S(1)}, ...), condition=%wide.region_3.4_spmd, body=%wide.region_1.3_spmd.sunk | while | flops 18612752 | bytes 5538680 | solution.py:77
  84.7 8.4 %collective-permute-done = bf16[16,8192]{1,0:T(8,128)(2,1)S(1)} collective-permute-done((bf16[16,8192]{1,0:T(8,128)(2,1)}, bf16[16,8192]{1,0:T(8,128)(2,1)S(1)}, u32[]{:S(2)}, u32[]{:S(2)}) %collective-permute-start) | collective-permute-done | bytes 262176 | tf_op jit(solution)/shard_map/while/body/eval_jaxpr/ppermute | solution.py:13
  99.3 7.5 %collective-permute-done = bf16[16,8192]{1,0:T(8,128)(2,1)S(1)} collective-permute-done((bf16[16,8192]{1,0:T(8,128)(2,1)}, bf16[16,8192]{1,0:T(8,128)(2,1)S(1)}, u32[]{:S(2)}, u32[]{:S(2)}) %collective-permute-start) | collective-permute-done | bytes 262176 | tf_op jit(solution)/shard_map/while/body/eval_jaxpr/ppermute | solution.py:13
  107.9 2.0 multiply_reduce_fusion.3
  113.0 6.7 %collective-permute-done = bf16[16,8192]{1,0:T(8,128)(2,1)S(1)} collective-permute-done((bf16[16,8192]{1,0:T(8,128)(2,1)}, bf16[16,8192]{1,0:T(8,128)(2,1)S(1)}, u32[]{:S(2)}, u32[]{:S(2)}) %collective-permute-start) | collective-permute-done | bytes 262176 | tf_op jit(solution)/shard_map/while/body/eval_jaxpr/ppermute | solution.py:13
  125.9 8.2 %collective-permute-done = bf16[16,8192]{1,0:T(8,128)(2,1)S(1)} collective-permute-done((bf16[16,8192]{1,0:T(8,128)(2,1)}, bf16[16,8192]{1,0:T(8,128)(2,1)S(1)}, u32[]{:S(2)}, u32[]{:S(2)}) %collective-permute-start) | collective-permute-done | bytes 262176 | tf_op jit(solution)/shard_map/while/body/eval_jaxpr/ppermute | solution.py:13
  140.3 6.4 %collective-permute-done = bf16[16,8192]{1,0:T(8,128)(2,1)S(1)} collective-permute-done((bf16[16,8192]{1,0:T(8,128)(2,1)}, bf16[16,8192]{1,0:T(8,128)(2,1)S(1)}, u32[]{:S(2)}, u32[]{:S(2)}) %collective-permute-start) | collective-permute-done | bytes 262176 | tf_op jit(solution)/shard_map/while/body/eval_jaxpr/ppermute | solution.py:13
  152.9 6.6 %collective-permute-done = bf16[16,8192]{1,0:T(8,128)(2,1)S(1)} collective-permute-done((bf16[16,8192]{1,0:T(8,128)(2,1)}, bf16[16,8192]{1,0:T(8,128)(2,1)S(1)}, u32[]{:S(2)}, u32[]{:S(2)}) %collective-permute-start) | collective-permute-done | bytes 262176 | tf_op jit(solution)/shard_map/while/body/eval_jaxpr/ppermute | solution.py:13
  165.7 7.2 %collective-permute-done = bf16[16,8192]{1,0:T(8,128)(2,1)S(1)} collective-permute-done((bf16[16,8192]{1,0:T(8,128)(2,1)}, bf16[16,8192]{1,0:T(8,128)(2,1)S(1)}, u32[]{:S(2)}, u32[]{:S(2)}) %collective-permute-start) | collective-permute-done | bytes 262176 | tf_op jit(solution)/shard_map/while/body/eval_jaxpr/ppermute | solution.py:13
  179.1 7.2 %collective-permute-done = bf16[16,8192]{1,0:T(8,128)(2,1)S(1)} collective-permute-done((bf16[16,8192]{1,0:T(8,128)(2,1)}, bf16[16,8192]{1,0:T(8,128)(2,1)S(1)}, u32[]{:S(2)}, u32[]{:S(2)}) %collective-permute-start) | collective-permute-done | bytes 262176 | tf_op jit(solution)/shard_map/while/body/eval_jaxpr/ppermute | solution.py:13
  192.5 7.2 %collective-permute-done = bf16[16,8192]{1,0:T(8,128)(2,1)S(1)} collective-permute-done((bf16[16,8192]{1,0:T(8,128)(2,1)}, bf16[16,8192]{1,0:T(8,128)(2,1)S(1)}, u32[]{:S(2)}, u32[]{:S(2)}) %collective-permute-start) | collective-permute-done | bytes 262176 | tf_op jit(solution)/shard_map/while/body/eval_jaxpr/ppermute | solution.py:13
  206.0 7.2 %collective-permute-done = bf16[16,8192]{1,0:T(8,128)(2,1)S(1)} collective-permute-done((bf16[16,8192]{1,0:T(8,128)(2,1)}, bf16[16,8192]{1,0:T(8,128)(2,1)S(1)}, u32[]{:S(2)}, u32[]{:S(2)}) %collective-permute-start) | collective-permute-done | bytes 262176 | tf_op jit(solution)/shard_map/while/body/eval_jaxpr/ppermute | solution.py:13
  219.4 7.2 %collective-permute-done = bf16[16,8192]{1,0:T(8,128)(2,1)S(1)} collective-permute-done((bf16[16,8192]{1,0:T(8,128)(2,1)}, bf16[16,8192]{1,0:T(8,128)(2,1)S(1)}, u32[]{:S(2)}, u32[]{:S(2)}) %collective-permute-start) | collective-permute-done | bytes 262176 | tf_op jit(solution)/shard_map/while/body/eval_jaxpr/ppermute | solution.py:13
  232.8 7.2 %collective-permute-done = bf16[16,8192]{1,0:T(8,128)(2,1)S(1)} collective-permute-done((bf16[16,8192]{1,0:T(8,128)(2,1)}, bf16[16,8192]{1,0:T(8,128)(2,1)S(1)}, u32[]{:S(2)}, u32[]{:S(2)}) %collective-permute-start) | collective-permute-done | bytes 262176 | tf_op jit(solution)/shard_map/while/body/eval_jaxpr/ppermute | solution.py:13
  246.3 8.4 %collective-permute-done = bf16[16,8192]{1,0:T(8,128)(2,1)S(1)} collective-permute-done((bf16[16,8192]{1,0:T(8,128)(2,1)}, bf16[16,8192]{1,0:T(8,128)(2,1)S(1)}, u32[]{:S(2)}, u32[]{:S(2)}) %collective-permute-start) | collective-permute-done | bytes 262176 | tf_op jit(solution)/shard_map/while/body/eval_jaxpr/ppermute | solution.py:13
  260.9 10.0 %collective-permute-done = bf16[16,8192]{1,0:T(8,128)(2,1)S(1)} collective-permute-done((bf16[16,8192]{1,0:T(8,128)(2,1)}, bf16[16,8192]{1,0:T(8,128)(2,1)S(1)}, u32[]{:S(2)}, u32[]{:S(2)}) %collective-permute-start) | collective-permute-done | bytes 262176 | tf_op jit(solution)/shard_map/while/body/eval_jaxpr/ppermute | solution.py:13
  277.1 10.7 %collective-permute-done = bf16[16,8192]{1,0:T(8,128)(2,1)S(1)} collective-permute-done((bf16[16,8192]{1,0:T(8,128)(2,1)}, bf16[16,8192]{1,0:T(8,128)(2,1)S(1)}, u32[]{:S(2)}, u32[]{:S(2)}) %collective-permute-start) | collective-permute-done | bytes 262176 | tf_op jit(solution)/shard_map/while/body/eval_jaxpr/ppermute | solution.py:13
  294.0 9.9 %collective-permute-done = bf16[16,8192]{1,0:T(8,128)(2,1)S(1)} collective-permute-done((bf16[16,8192]{1,0:T(8,128)(2,1)}, bf16[16,8192]{1,0:T(8,128)(2,1)S(1)}, u32[]{:S(2)}, u32[]{:S(2)}) %collective-permute-start) | collective-permute-done | bytes 262176 | tf_op jit(solution)/shard_map/while/body/eval_jaxpr/ppermute | solution.py:13
  310.1 7.9 %collective-permute-done = bf16[16,8192]{1,0:T(8,128)(2,1)S(1)} collective-permute-done((bf16[16,8192]{1,0:T(8,128)(2,1)}, bf16[16,8192]{1,0:T(8,128)(2,1)S(1)}, u32[]{:S(2)}, u32[]{:S(2)}) %collective-permute-start) | collective-permute-done | bytes 262176 | tf_op jit(solution)/shard_map/while/body/eval_jaxpr/ppermute | solution.py:13
  324.2 6.7 %collective-permute-done = bf16[16,8192]{1,0:T(8,128)(2,1)S(1)} collective-permute-done((bf16[16,8192]{1,0:T(8,128)(2,1)}, bf16[16,8192]{1,0:T(8,128)(2,1)S(1)}, u32[]{:S(2)}, u32[]{:S(2)}) %collective-permute-start) | collective-permute-done | bytes 262176 | tf_op jit(solution)/shard_map/while/body/eval_jaxpr/ppermute | solution.py:13
  337.1 6.4 %collective-permute-done = bf16[16,8192]{1,0:T(8,128)(2,1)S(1)} collective-permute-done((bf16[16,8192]{1,0:T(8,128)(2,1)}, bf16[16,8192]{1,0:T(8,128)(2,1)S(1)}, u32[]{:S(2)}, u32[]{:S(2)}) %collective-permute-start) | collective-permute-done | bytes 262176 | tf_op jit(solution)/shard_map/while/body/eval_jaxpr/ppermute | solution.py:13
  349.6 7.0 %collective-permute-done = bf16[16,8192]{1,0:T(8,128)(2,1)S(1)} collective-permute-done((bf16[16,8192]{1,0:T(8,128)(2,1)}, bf16[16,8192]{1,0:T(8,128)(2,1)S(1)}, u32[]{:S(2)}, u32[]{:S(2)}) %collective-permute-start) | collective-permute-done | bytes 262176 | tf_op jit(solution)/shard_map/while/body/eval_jaxpr/ppermute | solution.py:13
  362.8 7.2 %collective-permute-done = bf16[16,8192]{1,0:T(8,128)(2,1)S(1)} collective-permute-done((bf16[16,8192]{1,0:T(8,128)(2,1)}, bf16[16,8192]{1,0:T(8,128)(2,1)S(1)}, u32[]{:S(2)}, u32[]{:S(2)}) %collective-permute-start) | collective-permute-done | bytes 262176 | tf_op jit(solution)/shard_map/while/body/eval_jaxpr/ppermute | solution.py:13
  376.2 7.2 %collective-permute-done = bf16[16,8192]{1,0:T(8,128)(2,1)S(1)} collective-permute-done((bf16[16,8192]{1,0:T(8,128)(2,1)}, bf16[16,8192]{1,0:T(8,128)(2,1)S(1)}, u32[]{:S(2)}, u32[]{:S(2)}) %collective-permute-start) | collective-permute-done | bytes 262176 | tf_op jit(solution)/shard_map/while/body/eval_jaxpr/ppermute | solution.py:13
  389.7 7.2 %collective-permute-done = bf16[16,8192]{1,0:T(8,128)(2,1)S(1)} collective-permute-done((bf16[16,8192]{1,0:T(8,128)(2,1)}, bf16[16,8192]{1,0:T(8,128)(2,1)S(1)}, u32[]{:S(2)}, u32[]{:S(2)}) %collective-permute-start) | collective-permute-done | bytes 262176 | tf_op jit(solution)/shard_map/while/body/eval_jaxpr/ppermute | solution.py:13
  402.1 4.3 fusion.3
  406.4 2.5 fusion.2
  410.6 65.9 %reduce-scatter.2.cloned.1.call-done = f32[65,1024]{1,0:T(8,128)} async-done(((f32[65,8192]{1,0:T(8,128)}), f32[65,1024]{1,0:T(8,128)}) %reduce-scatter.2.cloned.1.call-update) | async-done | bytes 266256 | tf_op jit(solution)/shard_map/reduce_scatter | solution.py:89
  478.8 106.0 %psum.7 = f32[4]{0:T(128)S(1)} all-reduce(f32[4]{0:T(128)S(1)} %compare_select_fusion), channel_id=1, replica_groups=mesh['pipe'=16,'seq'=8,'dp'=4] {'pipe','seq','dp'}, use_global_device_ids=true, to_apply=%region_7.8 | all-reduce | flops 4 | bytes 32 | tf_op jit(solution)/shard_map/psum | solution.py:94
  (176 shorter events, 154.9 us)
Async XLA Ops:
  7.2 67.9 %all-gather.5.cloned.1.call-start = ((), (), s32[]{:S(2)}) async-start(), calls=%async_computation.1 | async-start | bytes 1216512 | tf_op jit(solution)/shard_map/all_gather | solution.py:23
  8.6 467.8 %reduce-scatter.2.cloned.1.call-start = ((), (), s32[]{:S(2)}) async-start(), calls=%async_computation.2 | async-start | bytes 2654208 | tf_op jit(solution)/shard_map/reduce_scatter | solution.py:89
  83.4 9.7 %collective-permute-start = (bf16[16,8192]{1,0:T(8,128)(2,1)}, bf16[16,8192]{1,0:T(8,128)(2,1)S(1)}, u32[]{:S(2)}, u32[]{:S(2)}) collective-permute-start(bf16[16,8192]{1,0:T(8,128)(2,1)} %add_convert_fusion.2), channel_id=1, source_target_pairs={{32,0},{64,32},{96,64},{128,96},{160,128},{192,160},{224,192},{256... | collective-permute-start | bytes 786440 | tf_op jit(solution)/shard_map/while/body/eval_jaxpr/ppermute | solution.py:13
  98.0 8.8 %collective-permute-start = (bf16[16,8192]{1,0:T(8,128)(2,1)}, bf16[16,8192]{1,0:T(8,128)(2,1)S(1)}, u32[]{:S(2)}, u32[]{:S(2)}) collective-permute-start(bf16[16,8192]{1,0:T(8,128)(2,1)} %add_convert_fusion.2), channel_id=1, source_target_pairs={{32,0},{64,32},{96,64},{128,96},{160,128},{192,160},{224,192},{256... | collective-permute-start | bytes 786440 | tf_op jit(solution)/shard_map/while/body/eval_jaxpr/ppermute | solution.py:13
  111.7 8.0 %collective-permute-start = (bf16[16,8192]{1,0:T(8,128)(2,1)}, bf16[16,8192]{1,0:T(8,128)(2,1)S(1)}, u32[]{:S(2)}, u32[]{:S(2)}) collective-permute-start(bf16[16,8192]{1,0:T(8,128)(2,1)} %add_convert_fusion.2), channel_id=1, source_target_pairs={{32,0},{64,32},{96,64},{128,96},{160,128},{192,160},{224,192},{256... | collective-permute-start | bytes 786440 | tf_op jit(solution)/shard_map/while/body/eval_jaxpr/ppermute | solution.py:13
  124.6 9.5 %collective-permute-start = (bf16[16,8192]{1,0:T(8,128)(2,1)}, bf16[16,8192]{1,0:T(8,128)(2,1)S(1)}, u32[]{:S(2)}, u32[]{:S(2)}) collective-permute-start(bf16[16,8192]{1,0:T(8,128)(2,1)} %add_convert_fusion.2), channel_id=1, source_target_pairs={{32,0},{64,32},{96,64},{128,96},{160,128},{192,160},{224,192},{256... | collective-permute-start | bytes 786440 | tf_op jit(solution)/shard_map/while/body/eval_jaxpr/ppermute | solution.py:13
  139.0 7.7 %collective-permute-start = (bf16[16,8192]{1,0:T(8,128)(2,1)}, bf16[16,8192]{1,0:T(8,128)(2,1)S(1)}, u32[]{:S(2)}, u32[]{:S(2)}) collective-permute-start(bf16[16,8192]{1,0:T(8,128)(2,1)} %add_convert_fusion.2), channel_id=1, source_target_pairs={{32,0},{64,32},{96,64},{128,96},{160,128},{192,160},{224,192},{256... | collective-permute-start | bytes 786440 | tf_op jit(solution)/shard_map/while/body/eval_jaxpr/ppermute | solution.py:13
  151.6 7.9 %collective-permute-start = (bf16[16,8192]{1,0:T(8,128)(2,1)}, bf16[16,8192]{1,0:T(8,128)(2,1)S(1)}, u32[]{:S(2)}, u32[]{:S(2)}) collective-permute-start(bf16[16,8192]{1,0:T(8,128)(2,1)} %add_convert_fusion.2), channel_id=1, source_target_pairs={{32,0},{64,32},{96,64},{128,96},{160,128},{192,160},{224,192},{256... | collective-permute-start | bytes 786440 | tf_op jit(solution)/shard_map/while/body/eval_jaxpr/ppermute | solution.py:13
  164.4 8.5 %collective-permute-start = (bf16[16,8192]{1,0:T(8,128)(2,1)}, bf16[16,8192]{1,0:T(8,128)(2,1)S(1)}, u32[]{:S(2)}, u32[]{:S(2)}) collective-permute-start(bf16[16,8192]{1,0:T(8,128)(2,1)} %add_convert_fusion.2), channel_id=1, source_target_pairs={{32,0},{64,32},{96,64},{128,96},{160,128},{192,160},{224,192},{256... | collective-permute-start | bytes 786440 | tf_op jit(solution)/shard_map/while/body/eval_jaxpr/ppermute | solution.py:13
  177.8 8.5 %collective-permute-start = (bf16[16,8192]{1,0:T(8,128)(2,1)}, bf16[16,8192]{1,0:T(8,128)(2,1)S(1)}, u32[]{:S(2)}, u32[]{:S(2)}) collective-permute-start(bf16[16,8192]{1,0:T(8,128)(2,1)} %add_convert_fusion.2), channel_id=1, source_target_pairs={{32,0},{64,32},{96,64},{128,96},{160,128},{192,160},{224,192},{256... | collective-permute-start | bytes 786440 | tf_op jit(solution)/shard_map/while/body/eval_jaxpr/ppermute | solution.py:13
  191.2 8.5 %collective-permute-start = (bf16[16,8192]{1,0:T(8,128)(2,1)}, bf16[16,8192]{1,0:T(8,128)(2,1)S(1)}, u32[]{:S(2)}, u32[]{:S(2)}) collective-permute-start(bf16[16,8192]{1,0:T(8,128)(2,1)} %add_convert_fusion.2), channel_id=1, source_target_pairs={{32,0},{64,32},{96,64},{128,96},{160,128},{192,160},{224,192},{256... | collective-permute-start | bytes 786440 | tf_op jit(solution)/shard_map/while/body/eval_jaxpr/ppermute | solution.py:13
  204.7 8.5 %collective-permute-start = (bf16[16,8192]{1,0:T(8,128)(2,1)}, bf16[16,8192]{1,0:T(8,128)(2,1)S(1)}, u32[]{:S(2)}, u32[]{:S(2)}) collective-permute-start(bf16[16,8192]{1,0:T(8,128)(2,1)} %add_convert_fusion.2), channel_id=1, source_target_pairs={{32,0},{64,32},{96,64},{128,96},{160,128},{192,160},{224,192},{256... | collective-permute-start | bytes 786440 | tf_op jit(solution)/shard_map/while/body/eval_jaxpr/ppermute | solution.py:13
  218.1 8.5 %collective-permute-start = (bf16[16,8192]{1,0:T(8,128)(2,1)}, bf16[16,8192]{1,0:T(8,128)(2,1)S(1)}, u32[]{:S(2)}, u32[]{:S(2)}) collective-permute-start(bf16[16,8192]{1,0:T(8,128)(2,1)} %add_convert_fusion.2), channel_id=1, source_target_pairs={{32,0},{64,32},{96,64},{128,96},{160,128},{192,160},{224,192},{256... | collective-permute-start | bytes 786440 | tf_op jit(solution)/shard_map/while/body/eval_jaxpr/ppermute | solution.py:13
  231.6 8.5 %collective-permute-start = (bf16[16,8192]{1,0:T(8,128)(2,1)}, bf16[16,8192]{1,0:T(8,128)(2,1)S(1)}, u32[]{:S(2)}, u32[]{:S(2)}) collective-permute-start(bf16[16,8192]{1,0:T(8,128)(2,1)} %add_convert_fusion.2), channel_id=1, source_target_pairs={{32,0},{64,32},{96,64},{128,96},{160,128},{192,160},{224,192},{256... | collective-permute-start | bytes 786440 | tf_op jit(solution)/shard_map/while/body/eval_jaxpr/ppermute | solution.py:13
  245.0 9.7 %collective-permute-start = (bf16[16,8192]{1,0:T(8,128)(2,1)}, bf16[16,8192]{1,0:T(8,128)(2,1)S(1)}, u32[]{:S(2)}, u32[]{:S(2)}) collective-permute-start(bf16[16,8192]{1,0:T(8,128)(2,1)} %add_convert_fusion.2), channel_id=1, source_target_pairs={{32,0},{64,32},{96,64},{128,96},{160,128},{192,160},{224,192},{256... | collective-permute-start | bytes 786440 | tf_op jit(solution)/shard_map/while/body/eval_jaxpr/ppermute | solution.py:13
  259.6 11.3 %collective-permute-start = (bf16[16,8192]{1,0:T(8,128)(2,1)}, bf16[16,8192]{1,0:T(8,128)(2,1)S(1)}, u32[]{:S(2)}, u32[]{:S(2)}) collective-permute-start(bf16[16,8192]{1,0:T(8,128)(2,1)} %add_convert_fusion.2), channel_id=1, source_target_pairs={{32,0},{64,32},{96,64},{128,96},{160,128},{192,160},{224,192},{256... | collective-permute-start | bytes 786440 | tf_op jit(solution)/shard_map/while/body/eval_jaxpr/ppermute | solution.py:13
  275.8 11.9 %collective-permute-start = (bf16[16,8192]{1,0:T(8,128)(2,1)}, bf16[16,8192]{1,0:T(8,128)(2,1)S(1)}, u32[]{:S(2)}, u32[]{:S(2)}) collective-permute-start(bf16[16,8192]{1,0:T(8,128)(2,1)} %add_convert_fusion.2), channel_id=1, source_target_pairs={{32,0},{64,32},{96,64},{128,96},{160,128},{192,160},{224,192},{256... | collective-permute-start | bytes 786440 | tf_op jit(solution)/shard_map/while/body/eval_jaxpr/ppermute | solution.py:13
  292.7 11.2 %collective-permute-start = (bf16[16,8192]{1,0:T(8,128)(2,1)}, bf16[16,8192]{1,0:T(8,128)(2,1)S(1)}, u32[]{:S(2)}, u32[]{:S(2)}) collective-permute-start(bf16[16,8192]{1,0:T(8,128)(2,1)} %add_convert_fusion.2), channel_id=1, source_target_pairs={{32,0},{64,32},{96,64},{128,96},{160,128},{192,160},{224,192},{256... | collective-permute-start | bytes 786440 | tf_op jit(solution)/shard_map/while/body/eval_jaxpr/ppermute | solution.py:13
  308.8 9.2 %collective-permute-start = (bf16[16,8192]{1,0:T(8,128)(2,1)}, bf16[16,8192]{1,0:T(8,128)(2,1)S(1)}, u32[]{:S(2)}, u32[]{:S(2)}) collective-permute-start(bf16[16,8192]{1,0:T(8,128)(2,1)} %add_convert_fusion.2), channel_id=1, source_target_pairs={{32,0},{64,32},{96,64},{128,96},{160,128},{192,160},{224,192},{256... | collective-permute-start | bytes 786440 | tf_op jit(solution)/shard_map/while/body/eval_jaxpr/ppermute | solution.py:13
  322.9 8.0 %collective-permute-start = (bf16[16,8192]{1,0:T(8,128)(2,1)}, bf16[16,8192]{1,0:T(8,128)(2,1)S(1)}, u32[]{:S(2)}, u32[]{:S(2)}) collective-permute-start(bf16[16,8192]{1,0:T(8,128)(2,1)} %add_convert_fusion.2), channel_id=1, source_target_pairs={{32,0},{64,32},{96,64},{128,96},{160,128},{192,160},{224,192},{256... | collective-permute-start | bytes 786440 | tf_op jit(solution)/shard_map/while/body/eval_jaxpr/ppermute | solution.py:13
  335.8 7.7 %collective-permute-start = (bf16[16,8192]{1,0:T(8,128)(2,1)}, bf16[16,8192]{1,0:T(8,128)(2,1)S(1)}, u32[]{:S(2)}, u32[]{:S(2)}) collective-permute-start(bf16[16,8192]{1,0:T(8,128)(2,1)} %add_convert_fusion.2), channel_id=1, source_target_pairs={{32,0},{64,32},{96,64},{128,96},{160,128},{192,160},{224,192},{256... | collective-permute-start | bytes 786440 | tf_op jit(solution)/shard_map/while/body/eval_jaxpr/ppermute | solution.py:13
  348.4 8.2 %collective-permute-start = (bf16[16,8192]{1,0:T(8,128)(2,1)}, bf16[16,8192]{1,0:T(8,128)(2,1)S(1)}, u32[]{:S(2)}, u32[]{:S(2)}) collective-permute-start(bf16[16,8192]{1,0:T(8,128)(2,1)} %add_convert_fusion.2), channel_id=1, source_target_pairs={{32,0},{64,32},{96,64},{128,96},{160,128},{192,160},{224,192},{256... | collective-permute-start | bytes 786440 | tf_op jit(solution)/shard_map/while/body/eval_jaxpr/ppermute | solution.py:13
  361.5 8.5 %collective-permute-start = (bf16[16,8192]{1,0:T(8,128)(2,1)}, bf16[16,8192]{1,0:T(8,128)(2,1)S(1)}, u32[]{:S(2)}, u32[]{:S(2)}) collective-permute-start(bf16[16,8192]{1,0:T(8,128)(2,1)} %add_convert_fusion.2), channel_id=1, source_target_pairs={{32,0},{64,32},{96,64},{128,96},{160,128},{192,160},{224,192},{256... | collective-permute-start | bytes 786440 | tf_op jit(solution)/shard_map/while/body/eval_jaxpr/ppermute | solution.py:13
  374.9 8.5 %collective-permute-start = (bf16[16,8192]{1,0:T(8,128)(2,1)}, bf16[16,8192]{1,0:T(8,128)(2,1)S(1)}, u32[]{:S(2)}, u32[]{:S(2)}) collective-permute-start(bf16[16,8192]{1,0:T(8,128)(2,1)} %add_convert_fusion.2), channel_id=1, source_target_pairs={{32,0},{64,32},{96,64},{128,96},{160,128},{192,160},{224,192},{256... | collective-permute-start | bytes 786440 | tf_op jit(solution)/shard_map/while/body/eval_jaxpr/ppermute | solution.py:13
  388.4 8.5 %collective-permute-start = (bf16[16,8192]{1,0:T(8,128)(2,1)}, bf16[16,8192]{1,0:T(8,128)(2,1)S(1)}, u32[]{:S(2)}, u32[]{:S(2)}) collective-permute-start(bf16[16,8192]{1,0:T(8,128)(2,1)} %add_convert_fusion.2), channel_id=1, source_target_pairs={{32,0},{64,32},{96,64},{128,96},{160,128},{192,160},{224,192},{256... | collective-permute-start | bytes 786440 | tf_op jit(solution)/shard_map/while/body/eval_jaxpr/ppermute | solution.py:13
  397.5 1.7 copy-start.3
  397.7 2.5 copy-start.2
  397.7 2.5 copy-start.7
  400.2 1.8 copy-start.1
  406.3 2.5 copy-start.4
  406.3 2.5 copy-start.5
  410.5 174.8 %all-gather.7.cloned.1.call-start = ((), (), s32[]{:S(2)}) async-start(), calls=%async_computation.3 | async-start | bytes 1474560 | tf_op jit(solution)/shard_map/all_gather | solution.py:97
  (2 other events, 1.9 us)
Sparse Core Ops, SparseCore 0:
  11.0 63.9 all-gather.4
  410.7 65.7 reduce-scatter.1
  478.6 31.4 all-gather.6
where the time goes:
time: 597 us; the launch traced here: 594 us
  waiting for transfers between devices  306 us (51%)
  blocking collectives  106 us (18%)
  other arithmetic  75.5 us (13%)
  matrix products  54.4 us (9%)
  starting transfers between devices  29.6 us (5%)
  between operations  13.9 us (2%)
  local copies, waits for them, and re-layouts  8.42 us (1%)
    ppermute x23, waiting for transfers between devices, from_behind(): lax.ppermute(value, axis, [(source, source + steps) for source in range(i...  176 us
    psum x1, blocking collectives, on_device(): totals = lax.psum(squares, ('pipe', 'seq', 'dp'))  106 us
    reduce_scatter x1, waiting for transfers between devices, on_device(): part = lax.psum_scatter(grads, 'seq', scatter_dimension=1, tiled=True)  65.9 us
    all_gather x1, waiting for transfers between devices, on_device(): whole = lax.all_gather(params, ('seq', 'dp'), axis=1, tiled=True)  64.3 us
    dot_general x23, matrix products, back_block(): jnp.dot(d_low, a_full, preferred_element_type=jnp.float32)  44.9 us
    convert_element_type x23, other arithmetic, back_block(): return hidden_gradient.astype(jnp.bfloat16)  42.7 us
    ppermute x23, starting transfers between devices, from_behind(): lax.ppermute(value, axis, [(source, source + steps) for source in range(i...  29.4 us
    dynamic_update_slice x23, other arithmetic, turn(): store = lax.dynamic_update_slice_in_dim(store, source[None], slot, 0)  23.3 us
  transfers between devices with their start and end apart: 26, of which 25 were waited for; matrix products, arithmetic and copies ran while one was open for 1% of the time, Pallas kernels for 0%

commit v1 on v0

--- a/solution.py
+++ b/solution.py
@@ -20,7 +20,10 @@
     top = top_grad[0]
     rank = a_rows.shape[1]
     params = jnp.concatenate([a_rows[0], b_rows[0], gain], axis=0)
-    whole = lax.all_gather(params, ("seq", "dp"), axis=1, tiled=True)
+    n_dev = lax.axis_size(("seq", "dp"))
+    blocks = jnp.stack([params for _ in range(n_dev)])
+    blocks = lax.all_to_all(blocks, ("seq", "dp"), split_axis=0, concat_axis=0)
+    whole = jnp.concatenate(blocks, axis=1)
     a_full = whole[:rank]
     b_full = whole[rank : 2 * rank]
     gain_float = whole[2 * rank].astype(jnp.float32)

time: 597 us -> 561 us (0.940)
  waiting for transfers between devices: 306 us -> 260 us
  starting transfers between devices: 29.6 us -> 40.6 us
    all_gather x1 -> x0, waiting for transfers between devices: 64.3 us -> none  [on_device(): whole = lax.all_gather(params, ('seq', 'dp'), axis=1, tiled=True)]
    all_to_all x0 -> x1, waiting for transfers between devices: none -> 16.9 us  [on_device(): blocks = lax.all_to_all(blocks, ('seq', 'dp'), split_axis=0, concat_axis=0)]
    all_to_all x0 -> x1, starting transfers between devices: none -> 11.1 us  [on_device(): blocks = lax.all_to_all(blocks, ('seq', 'dp'), split_axis=0, concat_axis=0)]
where the time goes in v1:
time: 561 us; the launch traced here: 558 us
  waiting for transfers between devices  260 us (46%)
  blocking collectives  106 us (19%)
  other arithmetic  74.8 us (13%)
  matrix products  52.6 us (9%)
  starting transfers between devices  40.6 us (7%)
  between operations  14.2 us (3%)
  local copies, waits for them, and re-layouts  9.58 us (2%)
    ppermute x23, waiting for transfers between devices, from_behind(): lax.ppermute(value, axis, [(source, source + steps) for source in range(i...  172 us
    psum x1, blocking collectives, on_device(): totals = lax.psum(squares, ('pipe', 'seq', 'dp'))  106 us
    reduce_scatter x1, waiting for transfers between devices, on_device(): part = lax.psum_scatter(grads, 'seq', scatter_dimension=1, tiled=True)  70.7 us
    dot_general x23, matrix products, back_block(): jnp.dot(d_low, a_full, preferred_element_type=jnp.float32)  44.9 us
    convert_element_type x23, other arithmetic, back_block(): return hidden_gradient.astype(jnp.bfloat16)  42.6 us
    ppermute x23, starting transfers between devices, from_behind(): lax.ppermute(value, axis, [(source, source + steps) for source in range(i...  29.4 us
    dynamic_update_slice x23, other arithmetic, turn(): store = lax.dynamic_update_slice_in_dim(store, source[None], slot, 0)  23.3 us
    all_to_all x1, waiting for transfers between devices, on_device(): blocks = lax.all_to_all(blocks, ('seq', 'dp'), split_axis=0, concat_axis=0)  16.9 us
  transfers between devices with their start and end apart: 26, of which 25 were waited for; matrix products, arithmetic and copies ran while one was open for 1% of the time, Pallas kernels for 0%

profile of v1, /device:TPU:1, one launch (start us, length us, event | category | flops | bytes accessed | tf_op | source)
XLA Modules:
  0.0 558.2 jit_solution(3656288521073063373)
XLA Ops:
  9.2 11.1 %all-to-all-start = ((bf16[32,65,256]{2,1,0:T(8,128)(2,1)}), bf16[32,65,256]{2,1,0:T(8,128)(2,1)}, u32[]{:S(2)}, u32[]{:S(2)}) async-start(bf16[32,65,256]{2,1,0:T(8,128)(2,1)} %stack.2), calls=%async_computation | async-start | bytes 2359296 | tf_op jit(solution)/shard_map/all_to_all | solution.py:25
  20.9 16.9 %all-to-all-done = bf16[32,65,256]{2,1,0:T(8,128)(2,1)} async-done(((bf16[32,65,256]{2,1,0:T(8,128)(2,1)}), bf16[32,65,256]{2,1,0:T(8,128)(2,1)}, u32[]{:S(2)}, u32[]{:S(2)}) %all-to-all-start) | async-done | bytes 1064992 | tf_op jit(solution)/shard_map/all_to_all | solution.py:25
  41.9 314.9 %while.17 = (s32[]{:T(128)}, bf16[16,8192]{1,0:T(8,128)(2,1)S(1)}, bf16[9,16,8192]{2,1,0:T(8,128)(2,1)S(1)}, pred[]{:T(512)}, s32[]{:T(128)}, /*index=5*/bf16[12...) while((s32[]{:T(128)}, bf16[16,8192]{1,0:T(8,128)(2,1)S(1)}, ...), condition=%wide.region_3.4_spmd, body=%wide.region_1.3_spmd.sunk | while | flops 18612752 | bytes 5538680 | solution.py:80
  48.2 7.4 %collective-permute-done = bf16[16,8192]{1,0:T(8,128)(2,1)S(1)} collective-permute-done((bf16[16,8192]{1,0:T(8,128)(2,1)}, bf16[16,8192]{1,0:T(8,128)(2,1)S(1)}, u32[]{:S(2)}, u32[]{:S(2)}) %collective-permute-start) | collective-permute-done | bytes 262176 | tf_op jit(solution)/shard_map/while/body/eval_jaxpr/ppermute | solution.py:13
  61.8 6.5 %collective-permute-done = bf16[16,8192]{1,0:T(8,128)(2,1)S(1)} collective-permute-done((bf16[16,8192]{1,0:T(8,128)(2,1)}, bf16[16,8192]{1,0:T(8,128)(2,1)S(1)}, u32[]{:S(2)}, u32[]{:S(2)}) %collective-permute-start) | collective-permute-done | bytes 262176 | tf_op jit(solution)/shard_map/while/body/eval_jaxpr/ppermute | solution.py:13
  74.5 6.0 %collective-permute-done = bf16[16,8192]{1,0:T(8,128)(2,1)S(1)} collective-permute-done((bf16[16,8192]{1,0:T(8,128)(2,1)}, bf16[16,8192]{1,0:T(8,128)(2,1)S(1)}, u32[]{:S(2)}, u32[]{:S(2)}) %collective-permute-start) | collective-permute-done | bytes 262176 | tf_op jit(solution)/shard_map/while/body/eval_jaxpr/ppermute | solution.py:13
  86.7 6.6 %collective-permute-done = bf16[16,8192]{1,0:T(8,128)(2,1)S(1)} collective-permute-done((bf16[16,8192]{1,0:T(8,128)(2,1)}, bf16[16,8192]{1,0:T(8,128)(2,1)S(1)}, u32[]{:S(2)}, u32[]{:S(2)}) %collective-permute-start) | collective-permute-done | bytes 262176 | tf_op jit(solution)/shard_map/while/body/eval_jaxpr/ppermute | solution.py:13
  99.5 6.5 %collective-permute-done = bf16[16,8192]{1,0:T(8,128)(2,1)S(1)} collective-permute-done((bf16[16,8192]{1,0:T(8,128)(2,1)}, bf16[16,8192]{1,0:T(8,128)(2,1)S(1)}, u32[]{:S(2)}, u32[]{:S(2)}) %collective-permute-start) | collective-permute-done | bytes 262176 | tf_op jit(solution)/shard_map/while/body/eval_jaxpr/ppermute | solution.py:13
  112.2 7.2 %collective-permute-done = bf16[16,8192]{1,0:T(8,128)(2,1)S(1)} collective-permute-done((bf16[16,8192]{1,0:T(8,128)(2,1)}, bf16[16,8192]{1,0:T(8,128)(2,1)S(1)}, u32[]{:S(2)}, u32[]{:S(2)}) %collective-permute-start) | collective-permute-done | bytes 262176 | tf_op jit(solution)/shard_map/while/body/eval_jaxpr/ppermute | solution.py:13
  120.5 2.0 multiply_reduce_fusion.3
  125.6 7.2 %collective-permute-done = bf16[16,8192]{1,0:T(8,128)(2,1)S(1)} collective-permute-done((bf16[16,8192]{1,0:T(8,128)(2,1)}, bf16[16,8192]{1,0:T(8,128)(2,1)S(1)}, u32[]{:S(2)}, u32[]{:S(2)}) %collective-permute-start) | collective-permute-done | bytes 262176 | tf_op jit(solution)/shard_map/while/body/eval_jaxpr/ppermute | solution.py:13
  139.0 7.2 %collective-permute-done = bf16[16,8192]{1,0:T(8,128)(2,1)S(1)} collective-permute-done((bf16[16,8192]{1,0:T(8,128)(2,1)}, bf16[16,8192]{1,0:T(8,128)(2,1)S(1)}, u32[]{:S(2)}, u32[]{:S(2)}) %collective-permute-start) | collective-permute-done | bytes 262176 | tf_op jit(solution)/shard_map/while/body/eval_jaxpr/ppermute | solution.py:13
  152.5 7.2 %collective-permute-done = bf16[16,8192]{1,0:T(8,128)(2,1)S(1)} collective-permute-done((bf16[16,8192]{1,0:T(8,128)(2,1)}, bf16[16,8192]{1,0:T(8,128)(2,1)S(1)}, u32[]{:S(2)}, u32[]{:S(2)}) %collective-permute-start) | collective-permute-done | bytes 262176 | tf_op jit(solution)/shard_map/while/body/eval_jaxpr/ppermute | solution.py:13
  165.9 7.2 %collective-permute-done = bf16[16,8192]{1,0:T(8,128)(2,1)S(1)} collective-permute-done((bf16[16,8192]{1,0:T(8,128)(2,1)}, bf16[16,8192]{1,0:T(8,128)(2,1)S(1)}, u32[]{:S(2)}, u32[]{:S(2)}) %collective-permute-start) | collective-permute-done | bytes 262176 | tf_op jit(solution)/shard_map/while/body/eval_jaxpr/ppermute | solution.py:13
  179.3 7.2 %collective-permute-done = bf16[16,8192]{1,0:T(8,128)(2,1)S(1)} collective-permute-done((bf16[16,8192]{1,0:T(8,128)(2,1)}, bf16[16,8192]{1,0:T(8,128)(2,1)S(1)}, u32[]{:S(2)}, u32[]{:S(2)}) %collective-permute-start) | collective-permute-done | bytes 262176 | tf_op jit(solution)/shard_map/while/body/eval_jaxpr/ppermute | solution.py:13
  192.8 8.3 %collective-permute-done = bf16[16,8192]{1,0:T(8,128)(2,1)S(1)} collective-permute-done((bf16[16,8192]{1,0:T(8,128)(2,1)}, bf16[16,8192]{1,0:T(8,128)(2,1)S(1)}, u32[]{:S(2)}, u32[]{:S(2)}) %collective-permute-start) | collective-permute-done | bytes 262176 | tf_op jit(solution)/shard_map/while/body/eval_jaxpr/ppermute | solution.py:13
  207.3 9.9 %collective-permute-done = bf16[16,8192]{1,0:T(8,128)(2,1)S(1)} collective-permute-done((bf16[16,8192]{1,0:T(8,128)(2,1)}, bf16[16,8192]{1,0:T(8,128)(2,1)S(1)}, u32[]{:S(2)}, u32[]{:S(2)}) %collective-permute-start) | collective-permute-done | bytes 262176 | tf_op jit(solution)/shard_map/while/body/eval_jaxpr/ppermute | solution.py:13
  223.4 10.7 %collective-permute-done = bf16[16,8192]{1,0:T(8,128)(2,1)S(1)} collective-permute-done((bf16[16,8192]{1,0:T(8,128)(2,1)}, bf16[16,8192]{1,0:T(8,128)(2,1)S(1)}, u32[]{:S(2)}, u32[]{:S(2)}) %collective-permute-start) | collective-permute-done | bytes 262176 | tf_op jit(solution)/shard_map/while/body/eval_jaxpr/ppermute | solution.py:13
  235.2 2.0 multiply_reduce_fusion.3
  240.3 9.8 %collective-permute-done = bf16[16,8192]{1,0:T(8,128)(2,1)S(1)} collective-permute-done((bf16[16,8192]{1,0:T(8,128)(2,1)}, bf16[16,8192]{1,0:T(8,128)(2,1)S(1)}, u32[]{:S(2)}, u32[]{:S(2)}) %collective-permute-start) | collective-permute-done | bytes 262176 | tf_op jit(solution)/shard_map/while/body/eval_jaxpr/ppermute | solution.py:13
  256.3 8.3 %collective-permute-done = bf16[16,8192]{1,0:T(8,128)(2,1)S(1)} collective-permute-done((bf16[16,8192]{1,0:T(8,128)(2,1)}, bf16[16,8192]{1,0:T(8,128)(2,1)S(1)}, u32[]{:S(2)}, u32[]{:S(2)}) %collective-permute-start) | collective-permute-done | bytes 262176 | tf_op jit(solution)/shard_map/while/body/eval_jaxpr/ppermute | solution.py:13
  270.7 6.8 %collective-permute-done = bf16[16,8192]{1,0:T(8,128)(2,1)S(1)} collective-permute-done((bf16[16,8192]{1,0:T(8,128)(2,1)}, bf16[16,8192]{1,0:T(8,128)(2,1)S(1)}, u32[]{:S(2)}, u32[]{:S(2)}) %collective-permute-start) | collective-permute-done | bytes 262176 | tf_op jit(solution)/shard_map/while/body/eval_jaxpr/ppermute | solution.py:13
  283.7 6.3 %collective-permute-done = bf16[16,8192]{1,0:T(8,128)(2,1)S(1)} collective-permute-done((bf16[16,8192]{1,0:T(8,128)(2,1)}, bf16[16,8192]{1,0:T(8,128)(2,1)S(1)}, u32[]{:S(2)}, u32[]{:S(2)}) %collective-permute-start) | collective-permute-done | bytes 262176 | tf_op jit(solution)/shard_map/while/body/eval_jaxpr/ppermute | solution.py:13
  296.2 7.0 %collective-permute-done = bf16[16,8192]{1,0:T(8,128)(2,1)S(1)} collective-permute-done((bf16[16,8192]{1,0:T(8,128)(2,1)}, bf16[16,8192]{1,0:T(8,128)(2,1)S(1)}, u32[]{:S(2)}, u32[]{:S(2)}) %collective-permute-start) | collective-permute-done | bytes 262176 | tf_op jit(solution)/shard_map/while/body/eval_jaxpr/ppermute | solution.py:13
  309.3 7.2 %collective-permute-done = bf16[16,8192]{1,0:T(8,128)(2,1)S(1)} collective-permute-done((bf16[16,8192]{1,0:T(8,128)(2,1)}, bf16[16,8192]{1,0:T(8,128)(2,1)S(1)}, u32[]{:S(2)}, u32[]{:S(2)}) %collective-permute-start) | collective-permute-done | bytes 262176 | tf_op jit(solution)/shard_map/while/body/eval_jaxpr/ppermute | solution.py:13
  322.8 7.2 %collective-permute-done = bf16[16,8192]{1,0:T(8,128)(2,1)S(1)} collective-permute-done((bf16[16,8192]{1,0:T(8,128)(2,1)}, bf16[16,8192]{1,0:T(8,128)(2,1)S(1)}, u32[]{:S(2)}, u32[]{:S(2)}) %collective-permute-start) | collective-permute-done | bytes 262176 | tf_op jit(solution)/shard_map/while/body/eval_jaxpr/ppermute | solution.py:13
  336.2 7.2 %collective-permute-done = bf16[16,8192]{1,0:T(8,128)(2,1)S(1)} collective-permute-done((bf16[16,8192]{1,0:T(8,128)(2,1)}, bf16[16,8192]{1,0:T(8,128)(2,1)S(1)}, u32[]{:S(2)}, u32[]{:S(2)}) %collective-permute-start) | collective-permute-done | bytes 262176 | tf_op jit(solution)/shard_map/while/body/eval_jaxpr/ppermute | solution.py:13
  349.6 7.2 %collective-permute-done = bf16[16,8192]{1,0:T(8,128)(2,1)S(1)} collective-permute-done((bf16[16,8192]{1,0:T(8,128)(2,1)}, bf16[16,8192]{1,0:T(8,128)(2,1)S(1)}, u32[]{:S(2)}, u32[]{:S(2)}) %collective-permute-start) | collective-permute-done | bytes 262176 | tf_op jit(solution)/shard_map/while/body/eval_jaxpr/ppermute | solution.py:13
  362.1 4.3 fusion.11
  366.4 3.1 pad_maximum_fusion
  369.6 70.7 %reduce-scatter.2.cloned.1.call-done = f32[65,1024]{1,0:T(8,128)} async-done(((f32[65,8192]{1,0:T(8,128)}), f32[65,1024]{1,0:T(8,128)}) %reduce-scatter.2.cloned.1.call-update) | async-done | bytes 266256 | tf_op jit(solution)/shard_map/reduce_scatter | solution.py:92
  442.6 105.9 %psum.7 = f32[4]{0:T(128)S(1)} all-reduce(f32[4]{0:T(128)S(1)} %compare_select_fusion), channel_id=1, replica_groups=mesh['pipe'=16,'seq'=8,'dp'=4] {'pipe','seq','dp'}, use_global_device_ids=true, to_apply=%region_7.8 | all-reduce | flops 4 | bytes 32 | tf_op jit(solution)/shard_map/psum | solution.py:97
  (172 shorter events, 155.3 us)
Async XLA Ops:
  7.2 13.2 %copy-start.1 = (bf16[1,1,128,8192]{3,2,1,0:T(8,128)(2,1)S(1)}, bf16[1,1,128,8192]{3,2,1,0:T(8,128)(2,1)}, u32[]{:S(2)}) copy-start(bf16[1,1,128,8192]{3,2,1,0:T(8,128)(2,1)} %param.7) | copy-start | bytes 6291460
  9.2 28.6 %all-to-all-start = ((bf16[32,65,256]{2,1,0:T(8,128)(2,1)}), bf16[32,65,256]{2,1,0:T(8,128)(2,1)}, u32[]{:S(2)}, u32[]{:S(2)}) async-start(bf16[32,65,256]{2,1,0:T(8,128)(2,1)} %stack.2), calls=%async_computation | async-start | bytes 2359296 | tf_op jit(solution)/shard_map/all_to_all | solution.py:25
  20.3 420.0 %reduce-scatter.2.cloned.1.call-start = ((), (), s32[]{:S(2)}) async-start(), calls=%async_computation.2 | async-start | bytes 2654208 | tf_op jit(solution)/shard_map/reduce_scatter | solution.py:92
  46.9 8.7 %collective-permute-start = (bf16[16,8192]{1,0:T(8,128)(2,1)}, bf16[16,8192]{1,0:T(8,128)(2,1)S(1)}, u32[]{:S(2)}, u32[]{:S(2)}) collective-permute-start(bf16[16,8192]{1,0:T(8,128)(2,1)} %add_convert_fusion.2), channel_id=1, source_target_pairs={{32,0},{64,32},{96,64},{128,96},{160,128},{192,160},{224,192},{256... | collective-permute-start | bytes 786440 | tf_op jit(solution)/shard_map/while/body/eval_jaxpr/ppermute | solution.py:13
  60.5 7.8 %collective-permute-start = (bf16[16,8192]{1,0:T(8,128)(2,1)}, bf16[16,8192]{1,0:T(8,128)(2,1)S(1)}, u32[]{:S(2)}, u32[]{:S(2)}) collective-permute-start(bf16[16,8192]{1,0:T(8,128)(2,1)} %add_convert_fusion.2), channel_id=1, source_target_pairs={{32,0},{64,32},{96,64},{128,96},{160,128},{192,160},{224,192},{256... | collective-permute-start | bytes 786440 | tf_op jit(solution)/shard_map/while/body/eval_jaxpr/ppermute | solution.py:13
  73.2 7.3 %collective-permute-start = (bf16[16,8192]{1,0:T(8,128)(2,1)}, bf16[16,8192]{1,0:T(8,128)(2,1)S(1)}, u32[]{:S(2)}, u32[]{:S(2)}) collective-permute-start(bf16[16,8192]{1,0:T(8,128)(2,1)} %add_convert_fusion.2), channel_id=1, source_target_pairs={{32,0},{64,32},{96,64},{128,96},{160,128},{192,160},{224,192},{256... | collective-permute-start | bytes 786440 | tf_op jit(solution)/shard_map/while/body/eval_jaxpr/ppermute | solution.py:13
  85.4 7.8 %collective-permute-start = (bf16[16,8192]{1,0:T(8,128)(2,1)}, bf16[16,8192]{1,0:T(8,128)(2,1)S(1)}, u32[]{:S(2)}, u32[]{:S(2)}) collective-permute-start(bf16[16,8192]{1,0:T(8,128)(2,1)} %add_convert_fusion.2), channel_id=1, source_target_pairs={{32,0},{64,32},{96,64},{128,96},{160,128},{192,160},{224,192},{256... | collective-permute-start | bytes 786440 | tf_op jit(solution)/shard_map/while/body/eval_jaxpr/ppermute | solution.py:13
  98.2 7.8 %collective-permute-start = (bf16[16,8192]{1,0:T(8,128)(2,1)}, bf16[16,8192]{1,0:T(8,128)(2,1)S(1)}, u32[]{:S(2)}, u32[]{:S(2)}) collective-permute-start(bf16[16,8192]{1,0:T(8,128)(2,1)} %add_convert_fusion.2), channel_id=1, source_target_pairs={{32,0},{64,32},{96,64},{128,96},{160,128},{192,160},{224,192},{256... | collective-permute-start | bytes 786440 | tf_op jit(solution)/shard_map/while/body/eval_jaxpr/ppermute | solution.py:13
  110.9 8.5 %collective-permute-start = (bf16[16,8192]{1,0:T(8,128)(2,1)}, bf16[16,8192]{1,0:T(8,128)(2,1)S(1)}, u32[]{:S(2)}, u32[]{:S(2)}) collective-permute-start(bf16[16,8192]{1,0:T(8,128)(2,1)} %add_convert_fusion.2), channel_id=1, source_target_pairs={{32,0},{64,32},{96,64},{128,96},{160,128},{192,160},{224,192},{256... | collective-permute-start | bytes 786440 | tf_op jit(solution)/shard_map/while/body/eval_jaxpr/ppermute | solution.py:13
  124.3 8.5 %collective-permute-start = (bf16[16,8192]{1,0:T(8,128)(2,1)}, bf16[16,8192]{1,0:T(8,128)(2,1)S(1)}, u32[]{:S(2)}, u32[]{:S(2)}) collective-permute-start(bf16[16,8192]{1,0:T(8,128)(2,1)} %add_convert_fusion.2), channel_id=1, source_target_pairs={{32,0},{64,32},{96,64},{128,96},{160,128},{192,160},{224,192},{256... | collective-permute-start | bytes 786440 | tf_op jit(solution)/shard_map/while/body/eval_jaxpr/ppermute | solution.py:13
  137.8 8.5 %collective-permute-start = (bf16[16,8192]{1,0:T(8,128)(2,1)}, bf16[16,8192]{1,0:T(8,128)(2,1)S(1)}, u32[]{:S(2)}, u32[]{:S(2)}) collective-permute-start(bf16[16,8192]{1,0:T(8,128)(2,1)} %add_convert_fusion.2), channel_id=1, source_target_pairs={{32,0},{64,32},{96,64},{128,96},{160,128},{192,160},{224,192},{256... | collective-permute-start | bytes 786440 | tf_op jit(solution)/shard_map/while/body/eval_jaxpr/ppermute | solution.py:13
  151.2 8.5 %collective-permute-start = (bf16[16,8192]{1,0:T(8,128)(2,1)}, bf16[16,8192]{1,0:T(8,128)(2,1)S(1)}, u32[]{:S(2)}, u32[]{:S(2)}) collective-permute-start(bf16[16,8192]{1,0:T(8,128)(2,1)} %add_convert_fusion.2), channel_id=1, source_target_pairs={{32,0},{64,32},{96,64},{128,96},{160,128},{192,160},{224,192},{256... | collective-permute-start | bytes 786440 | tf_op jit(solution)/shard_map/while/body/eval_jaxpr/ppermute | solution.py:13
  164.6 8.5 %collective-permute-start = (bf16[16,8192]{1,0:T(8,128)(2,1)}, bf16[16,8192]{1,0:T(8,128)(2,1)S(1)}, u32[]{:S(2)}, u32[]{:S(2)}) collective-permute-start(bf16[16,8192]{1,0:T(8,128)(2,1)} %add_convert_fusion.2), channel_id=1, source_target_pairs={{32,0},{64,32},{96,64},{128,96},{160,128},{192,160},{224,192},{256... | collective-permute-start | bytes 786440 | tf_op jit(solution)/shard_map/while/body/eval_jaxpr/ppermute | solution.py:13
  178.0 8.5 %collective-permute-start = (bf16[16,8192]{1,0:T(8,128)(2,1)}, bf16[16,8192]{1,0:T(8,128)(2,1)S(1)}, u32[]{:S(2)}, u32[]{:S(2)}) collective-permute-start(bf16[16,8192]{1,0:T(8,128)(2,1)} %add_convert_fusion.2), channel_id=1, source_target_pairs={{32,0},{64,32},{96,64},{128,96},{160,128},{192,160},{224,192},{256... | collective-permute-start | bytes 786440 | tf_op jit(solution)/shard_map/while/body/eval_jaxpr/ppermute | solution.py:13
  191.5 9.6 %collective-permute-start = (bf16[16,8192]{1,0:T(8,128)(2,1)}, bf16[16,8192]{1,0:T(8,128)(2,1)S(1)}, u32[]{:S(2)}, u32[]{:S(2)}) collective-permute-start(bf16[16,8192]{1,0:T(8,128)(2,1)} %add_convert_fusion.2), channel_id=1, source_target_pairs={{32,0},{64,32},{96,64},{128,96},{160,128},{192,160},{224,192},{256... | collective-permute-start | bytes 786440 | tf_op jit(solution)/shard_map/while/body/eval_jaxpr/ppermute | solution.py:13
  206.0 11.2 %collective-permute-start = (bf16[16,8192]{1,0:T(8,128)(2,1)}, bf16[16,8192]{1,0:T(8,128)(2,1)S(1)}, u32[]{:S(2)}, u32[]{:S(2)}) collective-permute-start(bf16[16,8192]{1,0:T(8,128)(2,1)} %add_convert_fusion.2), channel_id=1, source_target_pairs={{32,0},{64,32},{96,64},{128,96},{160,128},{192,160},{224,192},{256... | collective-permute-start | bytes 786440 | tf_op jit(solution)/shard_map/while/body/eval_jaxpr/ppermute | solution.py:13
  222.1 12.0 %collective-permute-start = (bf16[16,8192]{1,0:T(8,128)(2,1)}, bf16[16,8192]{1,0:T(8,128)(2,1)S(1)}, u32[]{:S(2)}, u32[]{:S(2)}) collective-permute-start(bf16[16,8192]{1,0:T(8,128)(2,1)} %add_convert_fusion.2), channel_id=1, source_target_pairs={{32,0},{64,32},{96,64},{128,96},{160,128},{192,160},{224,192},{256... | collective-permute-start | bytes 786440 | tf_op jit(solution)/shard_map/while/body/eval_jaxpr/ppermute | solution.py:13
  239.0 11.1 %collective-permute-start = (bf16[16,8192]{1,0:T(8,128)(2,1)}, bf16[16,8192]{1,0:T(8,128)(2,1)S(1)}, u32[]{:S(2)}, u32[]{:S(2)}) collective-permute-start(bf16[16,8192]{1,0:T(8,128)(2,1)} %add_convert_fusion.2), channel_id=1, source_target_pairs={{32,0},{64,32},{96,64},{128,96},{160,128},{192,160},{224,192},{256... | collective-permute-start | bytes 786440 | tf_op jit(solution)/shard_map/while/body/eval_jaxpr/ppermute | solution.py:13
  255.0 9.6 %collective-permute-start = (bf16[16,8192]{1,0:T(8,128)(2,1)}, bf16[16,8192]{1,0:T(8,128)(2,1)S(1)}, u32[]{:S(2)}, u32[]{:S(2)}) collective-permute-start(bf16[16,8192]{1,0:T(8,128)(2,1)} %add_convert_fusion.2), channel_id=1, source_target_pairs={{32,0},{64,32},{96,64},{128,96},{160,128},{192,160},{224,192},{256... | collective-permute-start | bytes 786440 | tf_op jit(solution)/shard_map/while/body/eval_jaxpr/ppermute | solution.py:13
  269.4 8.1 %collective-permute-start = (bf16[16,8192]{1,0:T(8,128)(2,1)}, bf16[16,8192]{1,0:T(8,128)(2,1)S(1)}, u32[]{:S(2)}, u32[]{:S(2)}) collective-permute-start(bf16[16,8192]{1,0:T(8,128)(2,1)} %add_convert_fusion.2), channel_id=1, source_target_pairs={{32,0},{64,32},{96,64},{128,96},{160,128},{192,160},{224,192},{256... | collective-permute-start | bytes 786440 | tf_op jit(solution)/shard_map/while/body/eval_jaxpr/ppermute | solution.py:13
  282.4 7.6 %collective-permute-start = (bf16[16,8192]{1,0:T(8,128)(2,1)}, bf16[16,8192]{1,0:T(8,128)(2,1)S(1)}, u32[]{:S(2)}, u32[]{:S(2)}) collective-permute-start(bf16[16,8192]{1,0:T(8,128)(2,1)} %add_convert_fusion.2), channel_id=1, source_target_pairs={{32,0},{64,32},{96,64},{128,96},{160,128},{192,160},{224,192},{256... | collective-permute-start | bytes 786440 | tf_op jit(solution)/shard_map/while/body/eval_jaxpr/ppermute | solution.py:13
  294.9 8.2 %collective-permute-start = (bf16[16,8192]{1,0:T(8,128)(2,1)}, bf16[16,8192]{1,0:T(8,128)(2,1)S(1)}, u32[]{:S(2)}, u32[]{:S(2)}) collective-permute-start(bf16[16,8192]{1,0:T(8,128)(2,1)} %add_convert_fusion.2), channel_id=1, source_target_pairs={{32,0},{64,32},{96,64},{128,96},{160,128},{192,160},{224,192},{256... | collective-permute-start | bytes 786440 | tf_op jit(solution)/shard_map/while/body/eval_jaxpr/ppermute | solution.py:13
  308.1 8.5 %collective-permute-start = (bf16[16,8192]{1,0:T(8,128)(2,1)}, bf16[16,8192]{1,0:T(8,128)(2,1)S(1)}, u32[]{:S(2)}, u32[]{:S(2)}) collective-permute-start(bf16[16,8192]{1,0:T(8,128)(2,1)} %add_convert_fusion.2), channel_id=1, source_target_pairs={{32,0},{64,32},{96,64},{128,96},{160,128},{192,160},{224,192},{256... | collective-permute-start | bytes 786440 | tf_op jit(solution)/shard_map/while/body/eval_jaxpr/ppermute | solution.py:13
  321.5 8.5 %collective-permute-start = (bf16[16,8192]{1,0:T(8,128)(2,1)}, bf16[16,8192]{1,0:T(8,128)(2,1)S(1)}, u32[]{:S(2)}, u32[]{:S(2)}) collective-permute-start(bf16[16,8192]{1,0:T(8,128)(2,1)} %add_convert_fusion.2), channel_id=1, source_target_pairs={{32,0},{64,32},{96,64},{128,96},{160,128},{192,160},{224,192},{256... | collective-permute-start | bytes 786440 | tf_op jit(solution)/shard_map/while/body/eval_jaxpr/ppermute | solution.py:13
  334.9 8.5 %collective-permute-start = (bf16[16,8192]{1,0:T(8,128)(2,1)}, bf16[16,8192]{1,0:T(8,128)(2,1)S(1)}, u32[]{:S(2)}, u32[]{:S(2)}) collective-permute-start(bf16[16,8192]{1,0:T(8,128)(2,1)} %add_convert_fusion.2), channel_id=1, source_target_pairs={{32,0},{64,32},{96,64},{128,96},{160,128},{192,160},{224,192},{256... | collective-permute-start | bytes 786440 | tf_op jit(solution)/shard_map/while/body/eval_jaxpr/ppermute | solution.py:13
  348.3 8.5 %collective-permute-start = (bf16[16,8192]{1,0:T(8,128)(2,1)}, bf16[16,8192]{1,0:T(8,128)(2,1)S(1)}, u32[]{:S(2)}, u32[]{:S(2)}) collective-permute-start(bf16[16,8192]{1,0:T(8,128)(2,1)} %add_convert_fusion.2), channel_id=1, source_target_pairs={{32,0},{64,32},{96,64},{128,96},{160,128},{192,160},{224,192},{256... | collective-permute-start | bytes 786440 | tf_op jit(solution)/shard_map/while/body/eval_jaxpr/ppermute | solution.py:13
  356.9 1.0 copy-start.3
  357.0 3.3 copy-start
  357.0 2.4 copy-start.2
  357.0 2.5 copy-start.4
  369.6 179.5 %all-gather.4.cloned.1.call-start = ((), (), s32[]{:S(2)}) async-start(), calls=%async_computation.3 | async-start | bytes 1474560 | tf_op jit(solution)/shard_map/all_gather | solution.py:100
Sparse Core Ops, SparseCore 0:
  369.7 70.5 reduce-scatter.1
  442.4 31.2 all-gather.3
